TPU v7x, 512 devices: a whole 4x8x8 slice. The times are simulated.
512 devices in a mesh: grp: 16 (over z, core), dev: 32 (over x, y).
Axes of the slice: x: 4, y: 8, z: 8, core: 2. Of those that a mesh axis runs over, the one named last changes fastest.
Arguments:
- ssm_input: bfloat16 [4096, 4096], P('grp', 'dev'), may hold values from -6 to 6
- gate_input: bfloat16 [4096, 4096], P('grp', 'dev'), may hold values from -6 to 6
- step_size: float32 [4096, 64], P('grp', 'dev'), may hold values from 6.1035156e-05 to 0.3375
- decay_rate: float32 [64], P('dev'), may hold values from 0.5 to 2
- in_coeff: bfloat16 [4096, 128], P('grp'), may hold values from -6 to 6
- out_coeff: bfloat16 [4096, 128], P('grp'), may hold values from -6 to 6
- skip_gain: float32 [64], P('dev'), may hold values from 0.5 to 3
- norm_gain: float32 [4096], P('dev'), may hold values from 0.5 to 1.5
- out_proj: bfloat16 [4096, 2048], P(None, 'dev'), may hold values from -0.09375 to 0.09375
- residual: bfloat16 [4096, 2048], P(('grp', 'dev')), may hold values from -6 to 6
- ffn_gain: float32 [2048], replicated, may hold values from 0.5 to 1.5
- router: float32 [2048, 16], replicated, may hold values from -0.125 to 0.125
- routes: int32 [4096, 2], P(('grp', 'dev')), may hold values from 0 to 15, all different within a row; in each aligned block of 8 rows (0 to 7, 8 to 15, ...) at most 2 rows name the same one
- gate_weight: bfloat16 [16, 2048, 8192], P('grp', None, 'dev'), may hold values from -0.125 to 0.125
- up_weight: bfloat16 [16, 2048, 8192], P('grp', None, 'dev'), may hold values from -0.125 to 0.125
- down_weight: bfloat16 [16, 8192, 2048], P('grp', 'dev'), may hold values from -0.0625 to 0.0625
Outputs:
- moe_out: bfloat16 [4096, 2048], P(('grp', 'dev'))
Inputs may be any that keep to these rules, and one draw needn't show every extreme that they name: `routes`: each row names two different experts; among the 8 rows of one dispatch block of consecutive tokens no expert is named more than 2 times, a bound that some block reaches.
All inputs are finite; a program needn't handle non-finite values.
Results may differ from a plain program's by a relative error of at most 0.012.
Values may be sent and summed in bfloat16 or wider, within the bound.
No kernel may reach another device: no remote copies, remote signals or barrier semaphores. Data moves between devices by JAX's collectives and lax.ppermute only.
A program may use at most 64 MiB of HBM per device.

v0:
```python
import jax
import jax.numpy as jnp
from jax import lax
from jax.sharding import Mesh
from jax.sharding import PartitionSpec as P

DEV = ("dev_0", "dev_1")
GRP_DEV = ("grp", "dev_0", "dev_1")
EPSILON = 1e-05
HIGHEST_PREC = lax.Precision.HIGHEST


def side_by_side(arrays, axis, dim, along):
    columns = [a.reshape(*a.shape[:along], -1) for a in arrays]
    both = jnp.concatenate(columns, axis=along)
    filled, at, finished = (lax.all_gather(both, axis, axis=dim, tiled=True), 0, [])
    for a, column in zip(arrays, columns):
        piece = filled[..., at : at + column.shape[along]]
        finished.append(piece.reshape(*piece.shape[:along], *a.shape[along:]))
        at += column.shape[along]
    return tuple(finished)


def sent_to_all(shard, axis):
    peers = lax.axis_size(axis)
    return lax.all_to_all(
        jnp.broadcast_to(shard[None], (peers, *shard.shape)), axis, 0, 0, tiled=True
    )


def of_everyone(shard, axis):
    everything = sent_to_all(shard, axis)
    return jnp.sum(everything, axis=0)


def in_order(tiles, dim):
    dims = list(tiles.shape[1:])
    dims[dim] *= tiles.shape[0]
    return jnp.moveaxis(tiles, 0, dim).reshape(dims)


def collect(shard, axis, dim):
    return in_order(sent_to_all(shard, axis), dim)


def sum_by_axis(terms, axes):
    total = terms.astype(jnp.bfloat16)
    total = lax.psum_scatter(total, axes, scatter_dimension=0, tiled=True)
    return total.astype(jnp.float32)


def rms_scale(values, gain_vec):
    return (
        values * lax.rsqrt(jnp.mean(values * values, axis=-1, keepdims=True) + EPSILON) * gain_vec
    )


def slot_tables(routes_block, expert_count, slot_cap):
    blocks, row_total = (routes_block.shape[0], routes_block.shape[1])
    flat_routes = routes_block.reshape(blocks, row_total * 2)
    onehot = (
        flat_routes[:, :, None] == jnp.arange(expert_count, dtype=jnp.int32)[None, None, :]
    ).astype(jnp.int32)
    earlier = jnp.cumsum(onehot, axis=1) - onehot
    slot_rank = jnp.sum(earlier * onehot, axis=2)
    slot_index = (flat_routes * slot_cap + slot_rank).reshape(blocks, row_total, 2)
    placed = (
        slot_index[:, :, :, None]
        == jnp.arange(expert_count * slot_cap, dtype=jnp.int32)[None, None, None, :]
    )
    return placed.astype(jnp.float32)


def shards(
    ssm_input,
    gate_input,
    step_size,
    decay_rate,
    in_coeff,
    out_coeff,
    skip_gain,
    norm_gain,
    out_proj,
    residual,
    ffn_gain,
    router,
    routes,
    gate_weight,
    up_weight,
    down_weight,
):
    tok_rows = ssm_input.shape[0]
    head_count = step_size.shape[1]
    head_width = ssm_input.shape[1] // head_count
    dev_count = lax.axis_size(DEV)
    inner_dim = ssm_input.shape[1] * dev_count
    block_rows = residual.shape[0]
    model_dim = residual.shape[1]
    experts = lax.axis_size("grp")
    slot_cap = max(2, 4 * block_rows // experts)
    group_slots = experts * slot_cap
    inputs_f = ssm_input.astype(jnp.float32).reshape(tok_rows, head_count, head_width)
    in_float = in_coeff.astype(jnp.float32)
    out_float = out_coeff.astype(jnp.float32)
    log_rate = -(step_size * decay_rate[None, :])
    cumulative = jnp.cumsum(log_rate, axis=0)
    causal = (jnp.arange(tok_rows)[:, None] >= jnp.arange(tok_rows)[None, :])[:, :, None]
    spread = cumulative[:, None, :] - cumulative[None, :, :]
    decay_pair = jnp.where(causal, jnp.exp(jnp.where(causal, spread, 0.0)), 0.0)
    scores = jnp.dot(out_coeff, in_coeff.T, preferred_element_type=jnp.float32)
    mixing = decay_pair * scores[:, :, None] * step_size[None, :, :]
    inside = jnp.einsum("tuh,uhp->thp", mixing, inputs_f, precision=HIGHEST_PREC)
    to_end = jnp.exp(cumulative[-1][None, :] - cumulative) * step_size
    own_state = jnp.einsum("uh,uhp,un->hpn", to_end, inputs_f, in_float, precision=HIGHEST_PREC)
    own_log = cumulative[-1]
    group_logs, group_states = tuple(
        (
            part.astype(jnp.float32)
            for part in side_by_side(
                (own_log[None].astype(jnp.bfloat16), own_state[None].astype(jnp.bfloat16)),
                "grp",
                0,
                2,
            )
        )
    )
    group_index = jnp.arange(group_logs.shape[0])
    my_group = lax.axis_index("grp")
    inclusive = jnp.cumsum(group_logs, axis=0)
    exclusive = inclusive - group_logs
    before_me = jnp.sum(jnp.where((group_index == my_group)[:, None], exclusive, 0.0), axis=0)
    earlier_mask = (group_index < my_group)[:, None]
    weighting = jnp.where(
        earlier_mask, jnp.exp(jnp.where(earlier_mask, before_me[None, :] - inclusive, 0.0)), 0.0
    )
    entering = jnp.einsum("gh,ghpn->hpn", weighting, group_states, precision=HIGHEST_PREC)
    carried = jnp.exp(cumulative)[:, :, None] * jnp.einsum(
        "hpn,tn->thp", entering, out_float, precision=HIGHEST_PREC
    )
    ssm_out = inside + carried + skip_gain[None, :, None] * inputs_f
    gated_out = ssm_out.reshape(tok_rows, head_count * head_width) * jax.nn.silu(
        gate_input.astype(jnp.float32)
    )
    squares = lax.psum(jnp.sum(gated_out * gated_out, axis=1), DEV)
    mixed_rows = (
        gated_out * lax.rsqrt(squares[:, None] / inner_dim + EPSILON) * norm_gain[None, :]
    ).astype(jnp.bfloat16)
    gathered = lax.all_gather(mixed_rows, DEV, axis=0)
    projected = jnp.einsum(
        "dtc,dcf->tf",
        gathered,
        out_proj.reshape(dev_count, -1, out_proj.shape[1]),
        preferred_element_type=jnp.float32,
    ).astype(jnp.bfloat16)
    mamba_out = lax.all_to_all(projected, DEV, split_axis=0, concat_axis=1, tiled=True)
    hidden_res = (residual.astype(jnp.float32) + mamba_out.astype(jnp.float32)).astype(jnp.bfloat16)
    hidden_float = hidden_res.astype(jnp.float32)
    normed = rms_scale(hidden_float, ffn_gain).astype(jnp.bfloat16)
    logits = jnp.dot(normed.astype(jnp.float32), router, precision=HIGHEST_PREC)
    expert_ids = jnp.arange(experts, dtype=jnp.int32)[None, :]
    first_logit = jnp.sum(logits * (routes[:, 0:1] == expert_ids).astype(jnp.float32), axis=1)
    second_logit = jnp.sum(logits * (routes[:, 1:2] == expert_ids).astype(jnp.float32), axis=1)
    first_prob = jax.nn.sigmoid(first_logit - second_logit)
    second_prob = 1.0 - first_prob
    placed = slot_tables(routes[None], experts, slot_cap)[0]
    filled = jnp.sum(placed, axis=1)
    outgoing = jnp.dot(
        filled.T.astype(jnp.bfloat16), normed, preferred_element_type=jnp.float32
    ).astype(jnp.bfloat16)
    outgoing = outgoing.reshape(experts, slot_cap, model_dim)
    arrived = lax.all_to_all(outgoing, "grp", split_axis=0, concat_axis=0, tiled=True)
    all_rows = lax.all_gather(arrived, DEV, axis=0, tiled=True).reshape(-1, model_dim)
    gate_act = jnp.dot(all_rows, gate_weight[0], preferred_element_type=jnp.float32)
    up_act = jnp.dot(all_rows, up_weight[0], preferred_element_type=jnp.float32)
    hidden = (jax.nn.silu(gate_act) * up_act).astype(jnp.bfloat16)
    summed = sum_by_axis(jnp.dot(hidden, down_weight[0], preferred_element_type=jnp.float32), DEV)
    returned = lax.all_to_all(
        summed.astype(jnp.bfloat16).reshape(experts, slot_cap, model_dim),
        "grp",
        split_axis=0,
        concat_axis=0,
        tiled=True,
    )
    weights = first_prob[:, None] * placed[:, 0, :] + second_prob[:, None] * placed[:, 1, :]
    contrib = jnp.dot(
        weights,
        returned.reshape(group_slots, model_dim).astype(jnp.float32),
        precision=HIGHEST_PREC,
    )
    return (hidden_float + contrib).astype(jnp.bfloat16)


def solution(mesh):
    torus = Mesh(mesh.devices.reshape(mesh.shape["grp"], 4, 8), ("grp", "dev_0", "dev_1"))
    in_specs = (
        P("grp", DEV),
        P("grp", DEV),
        P("grp", DEV),
        P(DEV),
        P("grp", None),
        P("grp", None),
        P(DEV),
        P(DEV),
        P(None, DEV),
        P(GRP_DEV, None),
        P(),
        P(),
        P(GRP_DEV, None),
        P("grp", None, DEV),
        P("grp", None, DEV),
        P("grp", DEV, None),
    )
    out_specs = P(GRP_DEV, None)
    return jax.shard_map(
        shards, mesh=torus, in_specs=in_specs, out_specs=out_specs, check_vma=False
    )
```

profile of v0, /device:TPU:1, one launch (start us, length us, event | category | flops | bytes accessed | tf_op | source)
XLA Modules:
  0.0 574.6 jit_solution(1486846018110611630)
XLA Ops:
  6.6 0.9 negate_bitcast_fusion
  8.8 0.8 fusion.58
  9.5 0.9 copy.61
  10.5 1.0 convolution_convert_fusion.2
  11.7 26.0 %all_gather.12 = bf16[16,2,8193]{2,1,0:T(2,128)(2,1)S(1)} all-gather(bf16[1,2,8193]{2,1,0:T(2,128)(2,1)S(1)} %pad_maximum_fusion), channel_id=1, replica_groups=mesh['grp'=16,'dev_0'=4,'dev_1'=8] {'grp'}, dimensions={0}, use_global_device_ids=true | all-gather | bytes 557124 | tf_op jit(solution)/shard_map/all_gather | solution.py:16
  37.6 0.7 slice.40
  39.3 1.1 fusion.59
  42.0 61.3 %psum.7 = f32[256]{0:T(256)S(1)} all-reduce(f32[256]{0:T(256)S(1)} %multiply_reduce_fusion), channel_id=1, replica_groups=mesh['grp'=16,'dev_0'=4,'dev_1'=8] {'dev_0','dev_1'}, use_global_device_ids=true, to_apply=%region_5.6 | all-reduce | flops 256 | bytes 2048 | tf_op jit(solution)/shard_map/psum | solution.py:144
  103.4 0.7 multiply_convert_fusion
  104.7 81.8 %all-gather.6.cloned.1.call-done = bf16[8192,128]{1,0:T(8,128)(2,1)} async-done(((bf16[256,128]{1,0:T(8,128)(2,1)}), bf16[8192,128]{1,0:T(8,128)(2,1)}) %all-gather.6.cloned.1.call-update) | async-done | bytes 2097168 | tf_op jit(solution)/shard_map/all_gather | solution.py:148
  186.6 2.3 fusion.5
  189.1 0.7 reshape.251
  189.8 4.9 all-to-all-start
  194.9 8.6 %all-to-all-done = bf16[32,2,256]{2,1,0:T(2,128)(2,1)S(1)} async-done(((bf16[32,2,256]{2,1,0:T(2,128)(2,1)}), bf16[32,2,256]{2,1,0:T(2,128)(2,1)S(1)}, u32[]{:S(2)}, u32[]{:S(2)}) %all-to-all-start) | async-done | bytes 32800 | tf_op jit(solution)/shard_map/all_to_all | solution.py:155
  204.3 22.8 %all_to_all.23 = bf16[16,2,2048]{2,1,0:T(2,128)(2,1)} all-to-all(bf16[16,2,2048]{2,1,0:T(2,128)(2,1)S(1)} %reshape.237), channel_id=1, replica_groups=mesh['grp'=16,'dev_0'=4,'dev_1'=8] {'grp'}, dimensions={0} | all-to-all | bytes 262144 | tf_op jit(solution)/shard_map/all_to_all | solution.py:171
  227.1 73.9 %all-gather.4.cloned.1.call-done = bf16[512,2,2048]{2,1,0:T(2,128)(2,1)} async-done(((bf16[16,2,2048]{2,1,0:T(2,128)(2,1)}), bf16[512,2,2048]{2,1,0:T(2,128)(2,1)}) %all-gather.4.cloned.1.call-update) | async-done | bytes 4194320 | tf_op jit(solution)/shard_map/all_gather | solution.py:172
  301.0 7.2 %reshape.238 = bf16[1024,2048]{1,0:T(8,128)(2,1)} reshape(bf16[512,2,2048]{2,1,0:T(2,128)(2,1)} %all-gather.4.cloned.1.call-done) | data formatting | bytes 8388608 | tf_op jit(solution)/shard_map/reshape | solution.py:172
  308.2 4.5 fusion.9
  312.8 9.1 %convolution_convert_fusion = bf16[1024,2048]{1,0:T(8,128)(2,1)} fusion(bf16[1024,2048]{1,0:T(8,128)(2,1)} %reshape.238, bf16[1,256,2048]{2,1,0:T(8,128)(2,1)S(1)} %copy-done, bf16[1,2048,256]{2,1,0:T(8,128)(2,1)} %param.30, f32[1024,256]{1,0:T(8,128)} %fusion.9), kind=kOutput, calls=%fused_computation | convolution fusion | flops 2151153664 | bytes 11534336 | tf_op jit(solution)/shard_map/dot_general | solution.py:176
  322.0 222.0 %reduce-scatter.2.cloned.1.call-done = bf16[32,2048]{1,0:T(8,128)(2,1)} async-done(((bf16[1024,2048]{1,0:T(8,128)(2,1)}), bf16[32,2048]{1,0:T(8,128)(2,1)}) %reduce-scatter.2.cloned.1.call-update) | async-done | bytes 131088 | tf_op jit(solution)/shard_map/reduce_scatter | solution.py:48
  544.0 1.7 reshape.239
  545.6 12.4 %all-to-all-start.2 = ((bf16[16,2,2048]{2,1,0:T(2,128)(2,1)}), bf16[16,2,2048]{2,1,0:T(2,128)(2,1)S(1)}, u32[]{:S(2)}, u32[]{:S(2)}) async-start(bf16[16,2,2048]{2,1,0:T(2,128)(2,1)} %reshape.239), calls=%async_computation.3 | async-start | bytes 262144 | tf_op jit(solution)/shard_map/all_to_all | solution.py:177
  558.4 8.8 %all-to-all-done.2 = bf16[16,2,2048]{2,1,0:T(2,128)(2,1)S(1)} async-done(((bf16[16,2,2048]{2,1,0:T(2,128)(2,1)}), bf16[16,2,2048]{2,1,0:T(2,128)(2,1)S(1)}, u32[]{:S(2)}, u32[]{:S(2)}) %all-to-all-start.2) | async-done | bytes 131104 | tf_op jit(solution)/shard_map/all_to_all | solution.py:177
  567.2 0.9 fusion
  (80 shorter events, 6.2 us)
Async XLA Ops:
  6.5 306.2 %copy-start = (bf16[1,256,2048]{2,1,0:T(8,128)(2,1)S(1)}, bf16[1,256,2048]{2,1,0:T(8,128)(2,1)}, u32[]{:S(2)}) copy-start(bf16[1,256,2048]{2,1,0:T(8,128)(2,1)} %param.31) | copy-start | bytes 3145732
  6.5 34.6 %copy-start.6 = (f32[256,2]{0,1:T(2,128)S(1)}, f32[256,2]{0,1:T(2,128)}, u32[]{:S(2)}) copy-start(f32[256,2]{0,1:T(2,128)} %param.18) | copy-start | bytes 6148
  6.5 34.4 %copy-start.3 = (bf16[256,128]{1,0:T(8,128)(2,1)S(1)}, bf16[256,128]{1,0:T(8,128)(2,1)}, u32[]{:S(2)}) copy-start(bf16[256,128]{1,0:T(8,128)(2,1)} %param.21) | copy-start | bytes 196612
  6.5 34.6 %copy-start.11 = (f32[2]{0:T(128)S(1)}, f32[2]{0:T(128)}, u32[]{:S(2)}) copy-start(f32[2]{0:T(128)} %param.22) | copy-start | bytes 28
  6.5 35.3 %copy-start.2 = (bf16[256,128]{1,0:T(8,128)(2,1)S(1)}, bf16[256,128]{1,0:T(8,128)(2,1)}, u32[]{:S(2)}) copy-start(bf16[256,128]{1,0:T(8,128)(2,1)} %param.17) | copy-start | bytes 196612
  6.5 96.8 %copy-start.8 = (f32[128]{0:T(128)S(1)}, f32[128]{0:T(128)}, u32[]{:S(2)}) copy-start(f32[128]{0:T(128)} %param.23) | copy-start | bytes 1540
  6.6 97.5 %copy-start.7 = (s32[8,2]{0,1:T(2,128)S(1)}, s32[8,2]{0,1:T(2,128)}, u32[]{:S(2)}) copy-start(s32[8,2]{0,1:T(2,128)} %param.28) | copy-start | bytes 196
  6.6 180.0 %copy-start.1 = (bf16[4096,64]{0,1:T(8,128)(2,1)S(1)}, bf16[4096,64]{0,1:T(8,128)(2,1)}, u32[]{:S(2)}) copy-start(bf16[4096,64]{0,1:T(8,128)(2,1)} %param.24) | copy-start | bytes 1572868
  6.6 180.0 %all-gather.6.cloned.1.call-start = ((), (), s32[]{:S(2)}) async-start(), calls=%async_computation.6 | async-start | bytes 2162688 | tf_op jit(solution)/shard_map/all_gather | solution.py:148
  38.3 165.4 %copy-start.4 = (bf16[8,2048]{1,0:T(8,128)(2,1)S(1)}, bf16[8,2048]{1,0:T(8,128)(2,1)}, u32[]{:S(2)}) copy-start(bf16[8,2048]{1,0:T(8,128)(2,1)} %param.25) | copy-start | bytes 98308
  38.7 165.2 %copy-start.5 = (f32[2048]{0:T(1024)S(1)}, f32[2048]{0:T(1024)}, u32[]{:S(2)}) copy-start(f32[2048]{0:T(1024)} %param.26) | copy-start | bytes 24580
  189.8 13.7 %all-to-all-start = ((bf16[32,2,256]{2,1,0:T(2,128)(2,1)}), bf16[32,2,256]{2,1,0:T(2,128)(2,1)S(1)}, u32[]{:S(2)}, u32[]{:S(2)}) async-start(bf16[32,2,256]{2,1,0:T(2,128)(2,1)} %reshape.251), calls=%async_computation | async-start | bytes 65536 | tf_op jit(solution)/shard_map/all_to_all | solution.py:155
  194.7 106.3 %all-gather.4.cloned.1.call-start = ((), (), s32[]{:S(2)}) async-start(), calls=%async_computation.4 | async-start | bytes 4325376 | tf_op jit(solution)/shard_map/all_gather | solution.py:172
  227.1 81.2 %copy-start.9 = (bf16[1,2048,256]{2,1,0:T(8,128)(2,1)S(1)}, bf16[1,2048,256]{2,1,0:T(8,128)(2,1)}, u32[]{:S(2)}) copy-start(bf16[1,2048,256]{2,1,0:T(8,128)(2,1)} %param.29) | copy-start | bytes 3145732
  227.1 316.9 %reduce-scatter.2.cloned.1.call-start = ((), (), s32[]{:S(2)}) async-start(), calls=%async_computation.5 | async-start | bytes 4325376 | tf_op jit(solution)/shard_map/reduce_scatter | solution.py:48
  321.9 236.1 %copy-start.10 = (f32[2048,16]{0,1:T(8,128)S(1)}, f32[2048,16]{0,1:T(8,128)}, u32[]{:S(2)}) copy-start(f32[2048,16]{0,1:T(8,128)} %param.27) | copy-start | bytes 393220
  545.6 21.6 %all-to-all-start.2 = ((bf16[16,2,2048]{2,1,0:T(2,128)(2,1)}), bf16[16,2,2048]{2,1,0:T(2,128)(2,1)S(1)}, u32[]{:S(2)}, u32[]{:S(2)}) async-start(bf16[16,2,2048]{2,1,0:T(2,128)(2,1)} %reshape.239), calls=%async_computation.3 | async-start | bytes 262144 | tf_op jit(solution)/shard_map/all_to_all | solution.py:177
Sparse Core Ops, SparseCore 0:
  104.2 82.3 all-gather.5
  227.2 73.7 all-gather.3
  322.0 221.9 reduce-scatter.1
where the time goes:
time: 575 us
  waiting for transfers between devices  395 us (69%)
  blocking collectives  110 us (19%)
  matrix products  20.9 us (4%)
  starting transfers between devices  17.4 us (3%)
  between operations  13.4 us (2%)
  local copies, waits for them, and re-layouts  13.3 us (2%)
    reduce_scatter x1, waiting for transfers between devices, sum_by_axis(): total = lax.psum_scatter(total, axes, scatter_dimension=0, tiled=True)  222 us
    all_gather x1, waiting for transfers between devices, shards(): gathered = lax.all_gather(mixed_rows, DEV, axis=0)  81.8 us
    all_gather x1, waiting for transfers between devices, shards(): lax.all_gather(arrived, DEV, axis=0, tiled=True).reshape(-1, model_dim)  73.9 us
    psum x1, blocking collectives, shards(): squares = lax.psum(jnp.sum(gated_out * gated_out, axis=1), DEV)  61.3 us
    all_gather x1, blocking collectives, side_by_side(): lax.all_gather(both, axis, axis=dim, tiled=True)  26 us
    all_to_all x1, blocking collectives, shards(): lax.all_to_all(outgoing, 'grp', split_axis=0, concat_axis=0, tiled=True)  22.8 us
    all_to_all x1, starting transfers between devices, shards(): lax.all_to_all(summed.astype(jnp.bfloat16).reshape(experts, slot_cap, mod...  12.4 us
  transfers between devices with their start and end apart: 5, of which 5 were waited for; matrix products, arithmetic and copies ran while one was open for 0% of the time, Pallas kernels for 0%

commit v1 on v0

--- a/solution.py
+++ b/solution.py
@@ -8,6 +8,11 @@
 GRP_DEV = ("grp", "dev_0", "dev_1")
 EPSILON = 1e-05
 HIGHEST_PREC = lax.Precision.HIGHEST
+
+
+def axis_by_axis(array, first, second):
+    half = lax.psum(array, first)
+    return lax.psum(half, second)
 
 
 def side_by_side(arrays, axis, dim, along):
@@ -141,7 +146,7 @@
     gated_out = ssm_out.reshape(tok_rows, head_count * head_width) * jax.nn.silu(
         gate_input.astype(jnp.float32)
     )
-    squares = lax.psum(jnp.sum(gated_out * gated_out, axis=1), DEV)
+    squares = axis_by_axis(jnp.sum(gated_out * gated_out, axis=1), "dev_1", "dev_0")
     mixed_rows = (
         gated_out * lax.rsqrt(squares[:, None] / inner_dim + EPSILON) * norm_gain[None, :]
     ).astype(jnp.bfloat16)

time: 575 us -> 531 us (0.923)
  blocking collectives: 110 us -> 71.1 us
    psum x1 -> x2, blocking collectives: 61.3 us -> 22.4 us  [the longest x1 13.9 us: axis_by_axis(): half = lax.psum(array, first)]
where the time goes in v1:
time: 531 us; the launch traced here: 530 us
  waiting for transfers between devices  390 us (73%)
  blocking collectives  71.1 us (13%)
  matrix products  20.9 us (4%)
  starting transfers between devices  17.5 us (3%)
  between operations  13.4 us (3%)
  local copies, waits for them, and re-layouts  13.3 us (3%)
    reduce_scatter x1, waiting for transfers between devices, sum_by_axis(): total = lax.psum_scatter(total, axes, scatter_dimension=0, tiled=True)  222 us
    all_gather x1, waiting for transfers between devices, shards(): gathered = lax.all_gather(mixed_rows, DEV, axis=0)  76.4 us
    all_gather x1, waiting for transfers between devices, shards(): lax.all_gather(arrived, DEV, axis=0, tiled=True).reshape(-1, model_dim)  73.9 us
    all_gather x1, blocking collectives, side_by_side(): lax.all_gather(both, axis, axis=dim, tiled=True)  26 us
    all_to_all x1, blocking collectives, shards(): lax.all_to_all(outgoing, 'grp', split_axis=0, concat_axis=0, tiled=True)  22.8 us
    psum x1, blocking collectives, axis_by_axis(): half = lax.psum(array, first)  13.9 us
    all_to_all x1, starting transfers between devices, shards(): lax.all_to_all(summed.astype(jnp.bfloat16).reshape(experts, slot_cap, mod...  12.4 us
  transfers between devices with their start and end apart: 5, of which 5 were waited for; matrix products, arithmetic and copies ran while one was open for 0% of the time, Pallas kernels for 0%

profile of v1, /device:TPU:1, one launch (start us, length us, event | category | flops | bytes accessed | tf_op | source)
XLA Modules:
  0.0 530.2 jit_solution(914711496053147012)
XLA Ops:
  6.6 0.9 negate_bitcast_fusion
  8.8 0.8 fusion.58
  9.5 0.9 copy.61
  10.5 1.0 convolution_convert_fusion.2
  11.7 26.0 %all_gather.12 = bf16[16,2,8193]{2,1,0:T(2,128)(2,1)S(1)} all-gather(bf16[1,2,8193]{2,1,0:T(2,128)(2,1)S(1)} %pad_maximum_fusion), channel_id=1, replica_groups=mesh['grp'=16,'dev_0'=4,'dev_1'=8] {'grp'}, dimensions={0}, use_global_device_ids=true | all-gather | bytes 557124 | tf_op jit(solution)/shard_map/all_gather | solution.py:21
  39.3 1.1 fusion.59
  42.0 13.9 %psum.14 = f32[256]{0:T(256)S(1)} all-reduce(f32[256]{0:T(256)S(1)} %multiply_reduce_fusion), channel_id=1, replica_groups=mesh['grp'=16,'dev_0'=4,'dev_1'=8] {'dev_1'}, use_global_device_ids=true, to_apply=%region_5.6 | all-reduce | flops 256 | bytes 2048 | tf_op jit(solution)/shard_map/psum | solution.py:14
  55.9 8.5 %psum.15 = f32[256]{0:T(256)S(1)} all-reduce(f32[256]{0:T(256)S(1)} %psum.14), channel_id=1, replica_groups=mesh['grp'=16,'dev_0'=4,'dev_1'=8] {'dev_0'}, use_global_device_ids=true, to_apply=%region_6.7 | all-reduce | flops 256 | bytes 2048 | tf_op jit(solution)/shard_map/psum | solution.py:15
  64.4 0.7 multiply_convert_fusion
  65.8 76.4 %all-gather.6.cloned.1.call-done = bf16[8192,128]{1,0:T(8,128)(2,1)} async-done(((bf16[256,128]{1,0:T(8,128)(2,1)}), bf16[8192,128]{1,0:T(8,128)(2,1)}) %all-gather.6.cloned.1.call-update) | async-done | bytes 2097168 | tf_op jit(solution)/shard_map/all_gather | solution.py:153
  142.2 2.3 fusion.5
  144.6 0.7 reshape.251
  145.4 4.9 all-to-all-start
  150.5 8.6 %all-to-all-done = bf16[32,2,256]{2,1,0:T(2,128)(2,1)S(1)} async-done(((bf16[32,2,256]{2,1,0:T(2,128)(2,1)}), bf16[32,2,256]{2,1,0:T(2,128)(2,1)S(1)}, u32[]{:S(2)}, u32[]{:S(2)}) %all-to-all-start) | async-done | bytes 32800 | tf_op jit(solution)/shard_map/all_to_all | solution.py:160
  159.9 22.8 %all_to_all.23 = bf16[16,2,2048]{2,1,0:T(2,128)(2,1)} all-to-all(bf16[16,2,2048]{2,1,0:T(2,128)(2,1)S(1)} %reshape.237), channel_id=1, replica_groups=mesh['grp'=16,'dev_0'=4,'dev_1'=8] {'grp'}, dimensions={0} | all-to-all | bytes 262144 | tf_op jit(solution)/shard_map/all_to_all | solution.py:176
  182.7 73.9 %all-gather.4.cloned.1.call-done = bf16[512,2,2048]{2,1,0:T(2,128)(2,1)} async-done(((bf16[16,2,2048]{2,1,0:T(2,128)(2,1)}), bf16[512,2,2048]{2,1,0:T(2,128)(2,1)}) %all-gather.4.cloned.1.call-update) | async-done | bytes 4194320 | tf_op jit(solution)/shard_map/all_gather | solution.py:177
  256.6 7.2 %reshape.238 = bf16[1024,2048]{1,0:T(8,128)(2,1)} reshape(bf16[512,2,2048]{2,1,0:T(2,128)(2,1)} %all-gather.4.cloned.1.call-done) | data formatting | bytes 8388608 | tf_op jit(solution)/shard_map/reshape | solution.py:177
  263.8 4.5 fusion.9
  268.3 9.1 %convolution_convert_fusion = bf16[1024,2048]{1,0:T(8,128)(2,1)} fusion(bf16[1024,2048]{1,0:T(8,128)(2,1)} %reshape.238, bf16[1,256,2048]{2,1,0:T(8,128)(2,1)S(1)} %copy-done, bf16[1,2048,256]{2,1,0:T(8,128)(2,1)} %param.30, f32[1024,256]{1,0:T(8,128)} %fusion.9), kind=kOutput, calls=%fused_computation | convolution fusion | flops 2151153664 | bytes 11534336 | tf_op jit(solution)/shard_map/dot_general | solution.py:181
  277.6 222.0 %reduce-scatter.2.cloned.1.call-done = bf16[32,2048]{1,0:T(8,128)(2,1)} async-done(((bf16[1024,2048]{1,0:T(8,128)(2,1)}), bf16[32,2048]{1,0:T(8,128)(2,1)}) %reduce-scatter.2.cloned.1.call-update) | async-done | bytes 131088 | tf_op jit(solution)/shard_map/reduce_scatter | solution.py:53
  499.5 1.7 reshape.239
  501.2 12.4 %all-to-all-start.2 = ((bf16[16,2,2048]{2,1,0:T(2,128)(2,1)}), bf16[16,2,2048]{2,1,0:T(2,128)(2,1)S(1)}, u32[]{:S(2)}, u32[]{:S(2)}) async-start(bf16[16,2,2048]{2,1,0:T(2,128)(2,1)} %reshape.239), calls=%async_computation.3 | async-start | bytes 262144 | tf_op jit(solution)/shard_map/all_to_all | solution.py:182
  514.0 8.8 %all-to-all-done.2 = bf16[16,2,2048]{2,1,0:T(2,128)(2,1)S(1)} async-done(((bf16[16,2,2048]{2,1,0:T(2,128)(2,1)}), bf16[16,2,2048]{2,1,0:T(2,128)(2,1)S(1)}, u32[]{:S(2)}, u32[]{:S(2)}) %all-to-all-start.2) | async-done | bytes 131104 | tf_op jit(solution)/shard_map/all_to_all | solution.py:182
  522.8 0.9 fusion
  (81 shorter events, 6.9 us)
Async XLA Ops:
  6.5 261.8 %copy-start = (bf16[1,256,2048]{2,1,0:T(8,128)(2,1)S(1)}, bf16[1,256,2048]{2,1,0:T(8,128)(2,1)}, u32[]{:S(2)}) copy-start(bf16[1,256,2048]{2,1,0:T(8,128)(2,1)} %param.31) | copy-start | bytes 3145732
  6.5 34.6 %copy-start.6 = (f32[256,2]{0,1:T(2,128)S(1)}, f32[256,2]{0,1:T(2,128)}, u32[]{:S(2)}) copy-start(f32[256,2]{0,1:T(2,128)} %param.18) | copy-start | bytes 6148
  6.5 34.4 %copy-start.3 = (bf16[256,128]{1,0:T(8,128)(2,1)S(1)}, bf16[256,128]{1,0:T(8,128)(2,1)}, u32[]{:S(2)}) copy-start(bf16[256,128]{1,0:T(8,128)(2,1)} %param.21) | copy-start | bytes 196612
  6.5 34.6 %copy-start.11 = (f32[2]{0:T(128)S(1)}, f32[2]{0:T(128)}, u32[]{:S(2)}) copy-start(f32[2]{0:T(128)} %param.22) | copy-start | bytes 28
  6.5 35.3 %copy-start.2 = (bf16[256,128]{1,0:T(8,128)(2,1)S(1)}, bf16[256,128]{1,0:T(8,128)(2,1)}, u32[]{:S(2)}) copy-start(bf16[256,128]{1,0:T(8,128)(2,1)} %param.17) | copy-start | bytes 196612
  6.5 57.9 %copy-start.8 = (f32[128]{0:T(128)S(1)}, f32[128]{0:T(128)}, u32[]{:S(2)}) copy-start(f32[128]{0:T(128)} %param.23) | copy-start | bytes 1540
  6.6 58.6 %copy-start.7 = (s32[8,2]{0,1:T(2,128)S(1)}, s32[8,2]{0,1:T(2,128)}, u32[]{:S(2)}) copy-start(s32[8,2]{0,1:T(2,128)} %param.28) | copy-start | bytes 196
  6.6 135.6 %copy-start.1 = (bf16[4096,64]{0,1:T(8,128)(2,1)S(1)}, bf16[4096,64]{0,1:T(8,128)(2,1)}, u32[]{:S(2)}) copy-start(bf16[4096,64]{0,1:T(8,128)(2,1)} %param.24) | copy-start | bytes 1572868
  6.6 135.6 %all-gather.6.cloned.1.call-start = ((), (), s32[]{:S(2)}) async-start(), calls=%async_computation.6 | async-start | bytes 2162688 | tf_op jit(solution)/shard_map/all_gather | solution.py:153
  38.3 121.0 %copy-start.4 = (bf16[8,2048]{1,0:T(8,128)(2,1)S(1)}, bf16[8,2048]{1,0:T(8,128)(2,1)}, u32[]{:S(2)}) copy-start(bf16[8,2048]{1,0:T(8,128)(2,1)} %param.25) | copy-start | bytes 98308
  38.7 120.8 %copy-start.5 = (f32[2048]{0:T(1024)S(1)}, f32[2048]{0:T(1024)}, u32[]{:S(2)}) copy-start(f32[2048]{0:T(1024)} %param.26) | copy-start | bytes 24580
  145.4 13.7 %all-to-all-start = ((bf16[32,2,256]{2,1,0:T(2,128)(2,1)}), bf16[32,2,256]{2,1,0:T(2,128)(2,1)S(1)}, u32[]{:S(2)}, u32[]{:S(2)}) async-start(bf16[32,2,256]{2,1,0:T(2,128)(2,1)} %reshape.251), calls=%async_computation | async-start | bytes 65536 | tf_op jit(solution)/shard_map/all_to_all | solution.py:160
  150.3 106.3 %all-gather.4.cloned.1.call-start = ((), (), s32[]{:S(2)}) async-start(), calls=%async_computation.4 | async-start | bytes 4325376 | tf_op jit(solution)/shard_map/all_gather | solution.py:177
  182.7 81.2 %copy-start.9 = (bf16[1,2048,256]{2,1,0:T(8,128)(2,1)S(1)}, bf16[1,2048,256]{2,1,0:T(8,128)(2,1)}, u32[]{:S(2)}) copy-start(bf16[1,2048,256]{2,1,0:T(8,128)(2,1)} %param.29) | copy-start | bytes 3145732
  182.7 316.9 %reduce-scatter.2.cloned.1.call-start = ((), (), s32[]{:S(2)}) async-start(), calls=%async_computation.5 | async-start | bytes 4325376 | tf_op jit(solution)/shard_map/reduce_scatter | solution.py:53
  277.4 236.1 %copy-start.10 = (f32[2048,16]{0,1:T(8,128)S(1)}, f32[2048,16]{0,1:T(8,128)}, u32[]{:S(2)}) copy-start(f32[2048,16]{0,1:T(8,128)} %param.27) | copy-start | bytes 393220
  501.2 21.6 %all-to-all-start.2 = ((bf16[16,2,2048]{2,1,0:T(2,128)(2,1)}), bf16[16,2,2048]{2,1,0:T(2,128)(2,1)S(1)}, u32[]{:S(2)}, u32[]{:S(2)}) async-start(bf16[16,2,2048]{2,1,0:T(2,128)(2,1)} %reshape.239), calls=%async_computation.3 | async-start | bytes 262144 | tf_op jit(solution)/shard_map/all_to_all | solution.py:182
Sparse Core Ops, SparseCore 0:
  65.3 76.8 all-gather.5
  182.8 73.7 all-gather.3
  277.6 221.9 reduce-scatter.1
